TPU v7x, 512 devices: a whole 4x8x8 slice. The times are simulated.
512 devices in a mesh: ind: 64 (over y, z), snp: 8 (over x, core).
Axes of the slice: x: 4, y: 8, z: 8, core: 2. Of those that a mesh axis runs over, the one named last changes fastest.
Arguments:
- genotypes: int32 [4096, 16384], P('ind', 'snp'), may hold values from 0 to 2
- observed: int32 [4096, 16384], P('ind', 'snp'), may hold values from 0 to 1
- ancestry: float32 [4096, 32], P('ind'), may hold values from 0.018 to 54.6, as said below
- freqs: float32 [16384, 32], P(('snp', 'ind')), may hold values from 0.05 to 0.95
Outputs:
- ancestry_out: float32 [4096, 32], P('ind')
- freqs_out: float32 [16384, 32], P(('snp', 'ind'))
Inputs may be any that keep to these rules, and one draw needn't show every extreme that they name: `ancestry`: positive weights.
All inputs are finite; a program needn't handle non-finite values.
Results may differ from a plain program's by a relative error of at most 0.0003.
Values sent between devices are 32-bit elements; how exact they have to be, the bound alone decides.
No kernel may reach another device: no remote copies, remote signals or barrier semaphores. Data moves between devices by JAX's collectives and lax.ppermute only.
A program may use at most 64 MiB of HBM per device.

v0:
```python
import jax
import jax.numpy as jnp
from jax import lax
from jax.sharding import PartitionSpec as P

STEPS = 3
clip_low = 1e-05
high = lax.Precision.HIGHEST


def over_rows(left, right):
    return lax.dot_general(
        left, right, (((0,), (0,)), ((), ())), precision=high, preferred_element_type=jnp.float32
    )


def per_device(genotypes, observed, ancestry, freqs):
    ind_count = lax.axis_size("ind")
    snp_count = lax.axis_size("snp")
    geno = genotypes.astype(jnp.float32)
    seen = observed.astype(jnp.float32)
    hits = seen * geno
    misses = seen * (2.0 - geno)
    own_rows = freqs.shape[0]
    q_zero = ancestry / jnp.sum(ancestry, axis=1, keepdims=True)
    f_zero = lax.all_gather(freqs, "ind", axis=0, tiled=True)
    f_weight = 1.0 / ind_count
    q_weight = 1.0 / snp_count

    def em_map(q_rows, f_state):
        prob = jnp.dot(q_rows, f_state.T, precision=high, preferred_element_type=jnp.float32)
        ratio_a = hits / prob
        ratio_b = misses / (1.0 - prob)
        sum_a = jnp.dot(ratio_a, f_state, precision=high, preferred_element_type=jnp.float32)
        sum_b = jnp.dot(ratio_b, 1.0 - f_state, precision=high, preferred_element_type=jnp.float32)
        c_part = over_rows(ratio_a, q_rows)
        d_part = over_rows(ratio_b, q_rows)
        sum_a, sum_b = lax.psum((sum_a, sum_b), "snp")
        q_next = q_rows * (sum_a + sum_b)
        q_next = q_next / jnp.sum(q_next, axis=1, keepdims=True)
        c_total, d_total = lax.psum((c_part, d_part), "ind")
        f_next = f_state * c_total / (f_state * c_total + (1.0 - f_state) * d_total)
        return (q_next, f_next)

    for step in range(STEPS):
        q_one, f_one = em_map(q_zero, f_zero)
        rq = q_one - q_zero
        rf = f_one - f_zero
        first_local = q_weight * jnp.sum(rq * rq) + f_weight * jnp.sum(rf * rf)
        q_two, f_two = em_map(q_one, f_one)
        vq = q_two - 2.0 * q_one + q_zero
        vf = f_two - 2.0 * f_one + f_zero
        second_local = q_weight * jnp.sum(vq * vq) + f_weight * jnp.sum(vf * vf)
        first, second = lax.psum((first_local, second_local), ("ind", "snp"))
        alpha = -jnp.sqrt(first / (second + 1e-20))
        q_ext = jnp.clip(q_zero - 2.0 * alpha * rq + alpha * alpha * vq, clip_low, 1.0 - clip_low)
        q_zero = q_ext / jnp.sum(q_ext, axis=1, keepdims=True)
        f_zero = jnp.clip(f_zero - 2.0 * alpha * rf + alpha * alpha * vf, clip_low, 1.0 - clip_low)
    f_final = lax.dynamic_slice_in_dim(f_zero, lax.axis_index("ind") * own_rows, own_rows, 0)
    return (q_zero, f_final)


def solution(mesh):
    in_specs = (P("ind", "snp"), P("ind", "snp"), P("ind", None), P(("snp", "ind"), None))
    out_specs = (P("ind", None), P(("snp", "ind"), None))
    return jax.shard_map(
        per_device, mesh=mesh, in_specs=in_specs, out_specs=out_specs, check_vma=False
    )
```

profile of v0, /device:TPU:1, one launch (start us, length us, event | category | flops | bytes accessed | tf_op | source)
XLA Modules:
  0.0 1308.1 jit_solution(10451656634871468365)
XLA Ops:
  7.2 47.0 %all_gather.3 = f32[2048,32]{1,0:T(8,128)S(1)} all-gather(f32[32,32]{1,0:T(8,128)} %param.7), channel_id=1, replica_groups=mesh['ind'=64,'snp'=8] {'ind'}, dimensions={0}, use_global_device_ids=true | all-gather | bytes 266240 | tf_op jit(solution)/shard_map/all_gather | solution.py:26
  54.3 1.3 fusion.48
  59.1 1.8 convolution_add_fusion
  60.9 32.1 %psum.240 = f32[64,32]{0,1:T(8,128)S(1)} all-reduce(f32[64,32]{0,1:T(8,128)S(1)} %convolution_add_fusion), channel_id=1, replica_groups=mesh['ind'=64,'snp'=8] {'snp'}, use_global_device_ids=true, to_apply=%region_1.0 | all-reduce | flops 2048 | bytes 16384 | tf_op jit(solution)/shard_map/psum | solution.py:38
  93.0 123.9 %all-reduce.26.cloned.1.call-done = (f32[2048,32]{0,1:T(8,128)}, f32[2048,32]{0,1:T(8,128)}) async-done(((f32[2048,32]{0,1:T(8,128)}, f32[2048,32]{0,1:T(8,128)}), (f32[2048,32]{0,1:T(8,128)}, f32[2048,32]{0,1:T(8,128)})) %all-reduce.26.cloned.1.call-update) | async-done | bytes 524304 | tf_op jit(solution)/shard_map/psum | solution.py:41
  216.9 1.7 multiply_reduce_fusion.5
  222.9 24.9 %psum.241 = f32[64,32]{0,1:T(8,128)S(1)} all-reduce(f32[64,32]{0,1:T(8,128)S(1)} %convolution_add_fusion.5), channel_id=1, replica_groups=mesh['ind'=64,'snp'=8] {'snp'}, use_global_device_ids=true, to_apply=%region_9.0 | all-reduce | flops 2048 | bytes 16384 | tf_op jit(solution)/shard_map/psum | solution.py:38
  250.5 123.8 %all-reduce.24.cloned.1.call-done = (f32[2048,32]{0,1:T(8,128)}, f32[2048,32]{0,1:T(8,128)}) async-done(((f32[2048,32]{0,1:T(8,128)}, f32[2048,32]{0,1:T(8,128)}), (f32[2048,32]{0,1:T(8,128)}, f32[2048,32]{0,1:T(8,128)})) %all-reduce.24.cloned.1.call-update) | async-done | bytes 524304 | tf_op jit(solution)/shard_map/psum | solution.py:41
  374.3 1.7 multiply_reduce_fusion.4
  376.7 99.3 %all-reduce.2 = (f32[]{:T(128)}, f32[]{:T(128)}) all-reduce(f32[]{:T(128)S(6)} %add.164, f32[]{:T(128)S(6)} %add.169), channel_id=1, replica_groups=mesh['ind'=64,'snp'=8] {'ind','snp'}, use_global_device_ids=true, to_apply=%region_8.0 | all-reduce | flops 2 | bytes 16 | tf_op jit(solution)/shard_map/psum | solution.py:54
  481.8 20.9 %psum.242 = f32[64,32]{0,1:T(8,128)S(1)} all-reduce(f32[64,32]{0,1:T(8,128)S(1)} %convolution_add_fusion.4), channel_id=1, replica_groups=mesh['ind'=64,'snp'=8] {'snp'}, use_global_device_ids=true, to_apply=%region_18.19 | all-reduce | flops 2048 | bytes 16384 | tf_op jit(solution)/shard_map/psum | solution.py:38
  502.7 125.4 %all-reduce.22.cloned.1.call-done = (f32[2048,32]{0,1:T(8,128)}, f32[2048,32]{0,1:T(8,128)}) async-done(((f32[2048,32]{0,1:T(8,128)}, f32[2048,32]{0,1:T(8,128)}), (f32[2048,32]{0,1:T(8,128)}, f32[2048,32]{0,1:T(8,128)})) %all-reduce.22.cloned.1.call-update) | async-done | bytes 524304 | tf_op jit(solution)/shard_map/psum | solution.py:41
  628.1 1.7 multiply_reduce_fusion.3
  634.8 24.9 %psum.243 = f32[64,32]{0,1:T(8,128)S(1)} all-reduce(f32[64,32]{0,1:T(8,128)S(1)} %convolution_add_fusion.3), channel_id=1, replica_groups=mesh['ind'=64,'snp'=8] {'snp'}, use_global_device_ids=true, to_apply=%region_26.27 | all-reduce | flops 2048 | bytes 16384 | tf_op jit(solution)/shard_map/psum | solution.py:38
  661.6 123.9 %all-reduce.20.cloned.1.call-done = (f32[2048,32]{0,1:T(8,128)}, f32[2048,32]{0,1:T(8,128)}) async-done(((f32[2048,32]{0,1:T(8,128)}, f32[2048,32]{0,1:T(8,128)}), (f32[2048,32]{0,1:T(8,128)}, f32[2048,32]{0,1:T(8,128)})) %all-reduce.20.cloned.1.call-update) | async-done | bytes 524304 | tf_op jit(solution)/shard_map/psum | solution.py:41
  785.6 1.7 multiply_reduce_fusion.2
  787.9 99.4 %all-reduce.1 = (f32[]{:T(128)}, f32[]{:T(128)}) all-reduce(f32[]{:T(128)S(6)} %add.175, f32[]{:T(128)S(6)} %add.180), channel_id=1, replica_groups=mesh['ind'=64,'snp'=8] {'ind','snp'}, use_global_device_ids=true, to_apply=%region_25.26 | all-reduce | flops 2 | bytes 16 | tf_op jit(solution)/shard_map/psum | solution.py:54
  893.1 20.8 %psum.244 = f32[64,32]{0,1:T(8,128)S(1)} all-reduce(f32[64,32]{0,1:T(8,128)S(1)} %convolution_add_fusion.2), channel_id=1, replica_groups=mesh['ind'=64,'snp'=8] {'snp'}, use_global_device_ids=true, to_apply=%region_35.36 | all-reduce | flops 2048 | bytes 16384 | tf_op jit(solution)/shard_map/psum | solution.py:38
  913.9 125.4 %all-reduce.18.cloned.1.call-done = (f32[2048,32]{0,1:T(8,128)}, f32[2048,32]{0,1:T(8,128)}) async-done(((f32[2048,32]{0,1:T(8,128)}, f32[2048,32]{0,1:T(8,128)}), (f32[2048,32]{0,1:T(8,128)}, f32[2048,32]{0,1:T(8,128)})) %all-reduce.18.cloned.1.call-update) | async-done | bytes 524304 | tf_op jit(solution)/shard_map/psum | solution.py:41
  1039.3 1.7 multiply_reduce_fusion.1
  1045.9 24.9 %psum.245 = f32[64,32]{0,1:T(8,128)S(1)} all-reduce(f32[64,32]{0,1:T(8,128)S(1)} %convolution_add_fusion.1), channel_id=1, replica_groups=mesh['ind'=64,'snp'=8] {'snp'}, use_global_device_ids=true, to_apply=%region_43.44 | all-reduce | flops 2048 | bytes 16384 | tf_op jit(solution)/shard_map/psum | solution.py:38
  1072.8 124.0 %all-reduce.16.cloned.1.call-done = (f32[2048,32]{0,1:T(8,128)}, f32[2048,32]{0,1:T(8,128)}) async-done(((f32[2048,32]{0,1:T(8,128)}, f32[2048,32]{0,1:T(8,128)}), (f32[2048,32]{0,1:T(8,128)}, f32[2048,32]{0,1:T(8,128)})) %all-reduce.16.cloned.1.call-update) | async-done | bytes 524304 | tf_op jit(solution)/shard_map/psum | solution.py:41
  1196.8 1.7 multiply_reduce_fusion
  1199.2 99.3 %all-reduce = (f32[]{:T(128)}, f32[]{:T(128)}) all-reduce(f32[]{:T(128)S(6)} %add.186, f32[]{:T(128)S(6)} %add.191), channel_id=1, replica_groups=mesh['ind'=64,'snp'=8] {'ind','snp'}, use_global_device_ids=true, to_apply=%region_42.43 | all-reduce | flops 2 | bytes 16 | tf_op jit(solution)/shard_map/psum | solution.py:54
  (66 shorter events, 28.6 us)
Async XLA Ops:
  7.2 47.0 %copy-start.2 = (f32[64,32]{0,1:T(8,128)S(1)}, f32[64,32]{0,1:T(8,128)}, u32[]{:S(2)}) copy-start(f32[64,32]{0,1:T(8,128)} %param.6) | copy-start | bytes 24580
  7.2 209.7 %all-reduce.26.cloned.1.call-start = ((), (), s32[]{:S(2)}) async-start(), calls=%async_computation.5 | async-start | bytes 1048576 | tf_op jit(solution)/shard_map/psum | solution.py:41
  54.2 1.3 copy-start
  54.2 1.3 copy-start.1
  58.2 316.1 %all-reduce.24.cloned.1.call-start = ((), (), s32[]{:S(2)}) async-start(), calls=%async_computation.4 | async-start | bytes 1048576 | tf_op jit(solution)/shard_map/psum | solution.py:41
  221.7 406.4 %all-reduce.22.cloned.1.call-start = ((), (), s32[]{:S(2)}) async-start(), calls=%async_computation.3 | async-start | bytes 1048576 | tf_op jit(solution)/shard_map/psum | solution.py:41
  480.6 305.0 %all-reduce.20.cloned.1.call-start = ((), (), s32[]{:S(2)}) async-start(), calls=%async_computation.2 | async-start | bytes 1048576 | tf_op jit(solution)/shard_map/psum | solution.py:41
  632.9 406.4 %all-reduce.18.cloned.1.call-start = ((), (), s32[]{:S(2)}) async-start(), calls=%async_computation.1 | async-start | bytes 1048576 | tf_op jit(solution)/shard_map/psum | solution.py:41
  891.8 304.9 %all-reduce.16.cloned.1.call-start = ((), (), s32[]{:S(2)}) async-start(), calls=%async_computation | async-start | bytes 1048576 | tf_op jit(solution)/shard_map/psum | solution.py:41
Sparse Core Ops, SparseCore 0:
  58.3 158.5 all-reduce.25
  221.8 152.4 all-reduce.23
  480.7 147.3 all-reduce.21
  633.0 152.4 all-reduce.19
  892.0 147.2 all-reduce.17
  1044.2 152.5 all-reduce.15
where the time goes:
time: 1310 us
  waiting for transfers between devices  746 us (57%)
  blocking collectives  494 us (38%)
  matrix products  27.2 us (2%)
  between operations  26.2 us (2%)
  other arithmetic  13.5 us (1%)
    psum x6, waiting for transfers between devices, em_map(): c_total, d_total = lax.psum((c_part, d_part), 'ind')  746 us
    psum x3, blocking collectives, per_device(): first, second = lax.psum((first_local, second_local), ('ind', 'snp'))  298 us
    psum x6, blocking collectives, em_map(): sum_a, sum_b = lax.psum((sum_a, sum_b), 'snp')  148 us
    all_gather x1, blocking collectives, per_device(): f_zero = lax.all_gather(freqs, 'ind', axis=0, tiled=True)  47 us
  transfers between devices with their start and end apart: 6, of which 6 were waited for; matrix products, arithmetic and copies ran while one was open for 1% of the time, Pallas kernels for 0%

commit v1 on v0

--- a/solution.py
+++ b/solution.py
@@ -23,7 +23,8 @@
     misses = seen * (2.0 - geno)
     own_rows = freqs.shape[0]
     q_zero = ancestry / jnp.sum(ancestry, axis=1, keepdims=True)
-    f_zero = lax.all_gather(freqs, "ind", axis=0, tiled=True)
+    repeated = jnp.stack([freqs] * lax.axis_size("ind"))
+    f_zero = jnp.concatenate(lax.all_to_all(repeated, "ind", 0, 0), axis=0)
     f_weight = 1.0 / ind_count
     q_weight = 1.0 / snp_count
 

time: 1310 us -> 1280 us (0.977)
  blocking collectives: 494 us -> 438 us
  starting transfers between devices: 0.25 us -> 17.7 us
    all_gather x1 -> x0, blocking collectives: 47 us -> none  [per_device(): f_zero = lax.all_gather(freqs, 'ind', axis=0, tiled=True)]
    all_to_all x0 -> x1, starting transfers between devices: none -> 17.3 us  [per_device(): f_zero = jnp.concatenate(lax.all_to_all(repeated, 'ind', 0, 0), axis=0)]
  transfers between devices with their start and end apart: 6 -> 7, of which waited for: 6 -> 7; matrix products, arithmetic and copies ran while one was open for 1% -> 1% of each run, Pallas kernels for 0% -> 0%
where the time goes in v1:
time: 1280 us
  waiting for transfers between devices  757 us (59%)
  blocking collectives  438 us (34%)
  between operations  26.3 us (2%)
  matrix products  25.3 us (2%)
  starting transfers between devices  17.7 us (1%)
  other arithmetic  14.8 us (1%)
    psum x6, waiting for transfers between devices, em_map(): c_total, d_total = lax.psum((c_part, d_part), 'ind')  744 us
    psum x3, blocking collectives, per_device(): first, second = lax.psum((first_local, second_local), ('ind', 'snp'))  298 us
    psum x6, blocking collectives, em_map(): sum_a, sum_b = lax.psum((sum_a, sum_b), 'snp')  140 us
  transfers between devices with their start and end apart: 7, of which 7 were waited for; matrix products, arithmetic and copies ran while one was open for 1% of the time, Pallas kernels for 0%

profile of v1, /device:TPU:1, one launch (start us, length us, event | category | flops | bytes accessed | tf_op | source)
XLA Modules:
  0.0 1283.5 jit_solution(10302896450984361995)
XLA Ops:
  9.3 17.3 %all-to-all-start = ((f32[64,1,1024]{2,1,0:T(1,128)}), f32[64,1,1024]{2,1,0:T(1,128)S(1)}, u32[]{:S(2)}, u32[]{:S(2)}) async-start(f32[64,1,1024]{2,1,0:T(1,128)} %reshape.20), calls=%async_computation | async-start | bytes 524288 | tf_op jit(solution)/shard_map/all_to_all | solution.py:27
  26.8 12.3 all-to-all-done
  39.6 1.3 reduce
  46.6 23.6 %psum.240 = f32[64,32]{0,1:T(8,128)S(1)} all-reduce(f32[64,32]{0,1:T(8,128)S(1)} %convolution_add_fusion.5), channel_id=1, replica_groups=mesh['ind'=64,'snp'=8] {'snp'}, use_global_device_ids=true, to_apply=%region_1.0 | all-reduce | flops 2048 | bytes 16384 | tf_op jit(solution)/shard_map/psum | solution.py:39
  70.2 122.0 %all-reduce.26.cloned.1.call-done = (f32[2048,32]{0,1:T(8,128)}, f32[2048,32]{0,1:T(8,128)}) async-done(((f32[2048,32]{0,1:T(8,128)}, f32[2048,32]{0,1:T(8,128)}), (f32[2048,32]{0,1:T(8,128)}, f32[2048,32]{0,1:T(8,128)})) %all-reduce.26.cloned.1.call-update) | async-done | bytes 524304 | tf_op jit(solution)/shard_map/psum | solution.py:42
  192.3 1.7 multiply_reduce_fusion.5
  198.3 24.9 %psum.241 = f32[64,32]{0,1:T(8,128)S(1)} all-reduce(f32[64,32]{0,1:T(8,128)S(1)} %convolution_add_fusion.4), channel_id=1, replica_groups=mesh['ind'=64,'snp'=8] {'snp'}, use_global_device_ids=true, to_apply=%region_9.0 | all-reduce | flops 2048 | bytes 16384 | tf_op jit(solution)/shard_map/psum | solution.py:39
  225.9 123.8 %all-reduce.24.cloned.1.call-done = (f32[2048,32]{0,1:T(8,128)}, f32[2048,32]{0,1:T(8,128)}) async-done(((f32[2048,32]{0,1:T(8,128)}, f32[2048,32]{0,1:T(8,128)}), (f32[2048,32]{0,1:T(8,128)}, f32[2048,32]{0,1:T(8,128)})) %all-reduce.24.cloned.1.call-update) | async-done | bytes 524304 | tf_op jit(solution)/shard_map/psum | solution.py:42
  349.7 1.7 multiply_reduce_fusion.4
  352.1 99.4 %all-reduce.2 = (f32[]{:T(128)}, f32[]{:T(128)}) all-reduce(f32[]{:T(128)S(6)} %add.164, f32[]{:T(128)S(6)} %add.169), channel_id=1, replica_groups=mesh['ind'=64,'snp'=8] {'ind','snp'}, use_global_device_ids=true, to_apply=%region_8.0 | all-reduce | flops 2 | bytes 16 | tf_op jit(solution)/shard_map/psum | solution.py:55
  457.4 20.8 %psum.242 = f32[64,32]{0,1:T(8,128)S(1)} all-reduce(f32[64,32]{0,1:T(8,128)S(1)} %convolution_add_fusion.3), channel_id=1, replica_groups=mesh['ind'=64,'snp'=8] {'snp'}, use_global_device_ids=true, to_apply=%region_18.19 | all-reduce | flops 2048 | bytes 16384 | tf_op jit(solution)/shard_map/psum | solution.py:39
  478.2 125.2 %all-reduce.22.cloned.1.call-done = (f32[2048,32]{0,1:T(8,128)}, f32[2048,32]{0,1:T(8,128)}) async-done(((f32[2048,32]{0,1:T(8,128)}, f32[2048,32]{0,1:T(8,128)}), (f32[2048,32]{0,1:T(8,128)}, f32[2048,32]{0,1:T(8,128)})) %all-reduce.22.cloned.1.call-update) | async-done | bytes 524304 | tf_op jit(solution)/shard_map/psum | solution.py:42
  603.5 1.7 multiply_reduce_fusion.3
  610.2 24.9 %psum.243 = f32[64,32]{0,1:T(8,128)S(1)} all-reduce(f32[64,32]{0,1:T(8,128)S(1)} %convolution_add_fusion.2), channel_id=1, replica_groups=mesh['ind'=64,'snp'=8] {'snp'}, use_global_device_ids=true, to_apply=%region_26.27 | all-reduce | flops 2048 | bytes 16384 | tf_op jit(solution)/shard_map/psum | solution.py:39
  637.0 123.9 %all-reduce.20.cloned.1.call-done = (f32[2048,32]{0,1:T(8,128)}, f32[2048,32]{0,1:T(8,128)}) async-done(((f32[2048,32]{0,1:T(8,128)}, f32[2048,32]{0,1:T(8,128)}), (f32[2048,32]{0,1:T(8,128)}, f32[2048,32]{0,1:T(8,128)})) %all-reduce.20.cloned.1.call-update) | async-done | bytes 524304 | tf_op jit(solution)/shard_map/psum | solution.py:42
  760.9 1.7 multiply_reduce_fusion.2
  763.3 99.4 %all-reduce.1 = (f32[]{:T(128)}, f32[]{:T(128)}) all-reduce(f32[]{:T(128)S(6)} %add.175, f32[]{:T(128)S(6)} %add.180), channel_id=1, replica_groups=mesh['ind'=64,'snp'=8] {'ind','snp'}, use_global_device_ids=true, to_apply=%region_25.26 | all-reduce | flops 2 | bytes 16 | tf_op jit(solution)/shard_map/psum | solution.py:55
  868.4 20.8 %psum.244 = f32[64,32]{0,1:T(8,128)S(1)} all-reduce(f32[64,32]{0,1:T(8,128)S(1)} %convolution_add_fusion.1), channel_id=1, replica_groups=mesh['ind'=64,'snp'=8] {'snp'}, use_global_device_ids=true, to_apply=%region_35.36 | all-reduce | flops 2048 | bytes 16384 | tf_op jit(solution)/shard_map/psum | solution.py:39
  889.2 125.5 %all-reduce.18.cloned.1.call-done = (f32[2048,32]{0,1:T(8,128)}, f32[2048,32]{0,1:T(8,128)}) async-done(((f32[2048,32]{0,1:T(8,128)}, f32[2048,32]{0,1:T(8,128)}), (f32[2048,32]{0,1:T(8,128)}, f32[2048,32]{0,1:T(8,128)})) %all-reduce.18.cloned.1.call-update) | async-done | bytes 524304 | tf_op jit(solution)/shard_map/psum | solution.py:42
  1014.7 1.7 multiply_reduce_fusion.1
  1021.3 24.9 %psum.245 = f32[64,32]{0,1:T(8,128)S(1)} all-reduce(f32[64,32]{0,1:T(8,128)S(1)} %convolution_add_fusion), channel_id=1, replica_groups=mesh['ind'=64,'snp'=8] {'snp'}, use_global_device_ids=true, to_apply=%region_43.44 | all-reduce | flops 2048 | bytes 16384 | tf_op jit(solution)/shard_map/psum | solution.py:39
  1048.2 123.9 %all-reduce.16.cloned.1.call-done = (f32[2048,32]{0,1:T(8,128)}, f32[2048,32]{0,1:T(8,128)}) async-done(((f32[2048,32]{0,1:T(8,128)}, f32[2048,32]{0,1:T(8,128)}), (f32[2048,32]{0,1:T(8,128)}, f32[2048,32]{0,1:T(8,128)})) %all-reduce.16.cloned.1.call-update) | async-done | bytes 524304 | tf_op jit(solution)/shard_map/psum | solution.py:42
  1172.1 1.7 multiply_reduce_fusion
  1174.5 99.4 %all-reduce = (f32[]{:T(128)}, f32[]{:T(128)}) all-reduce(f32[]{:T(128)S(6)} %add.186, f32[]{:T(128)S(6)} %add.191), channel_id=1, replica_groups=mesh['ind'=64,'snp'=8] {'ind','snp'}, use_global_device_ids=true, to_apply=%region_42.43 | all-reduce | flops 2 | bytes 16 | tf_op jit(solution)/shard_map/psum | solution.py:55
  (74 shorter events, 33.7 us)
Async XLA Ops:
  8.1 18.5 %copy-start.2 = (f32[64,32]{0,1:T(8,128)S(1)}, f32[64,32]{0,1:T(8,128)}, u32[]{:S(2)}) copy-start(f32[64,32]{0,1:T(8,128)} %param.6) | copy-start | bytes 24580
  8.1 18.5 %copy-start.1 = (s32[64,2048]{1,0:T(8,128)S(1)}, s32[64,2048]{1,0:T(8,128)}, u32[]{:S(2)}) copy-start(s32[64,2048]{1,0:T(8,128)} %param.5) | copy-start | bytes 1572868
  9.3 17.4 %copy-start = (s32[64,2048]{1,0:T(8,128)S(1)}, s32[64,2048]{1,0:T(8,128)}, u32[]{:S(2)}) copy-start(s32[64,2048]{1,0:T(8,128)} %param.4) | copy-start | bytes 1572868
  9.3 29.8 %all-to-all-start = ((f32[64,1,1024]{2,1,0:T(1,128)}), f32[64,1,1024]{2,1,0:T(1,128)S(1)}, u32[]{:S(2)}, u32[]{:S(2)}) async-start(f32[64,1,1024]{2,1,0:T(1,128)} %reshape.20), calls=%async_computation | async-start | bytes 524288 | tf_op jit(solution)/shard_map/all_to_all | solution.py:27
  26.5 165.7 %all-reduce.26.cloned.1.call-start = ((), (), s32[]{:S(2)}) async-start(), calls=%async_computation.6 | async-start | bytes 1048576 | tf_op jit(solution)/shard_map/psum | solution.py:42
  45.4 304.3 %all-reduce.24.cloned.1.call-start = ((), (), s32[]{:S(2)}) async-start(), calls=%async_computation.5 | async-start | bytes 1048576 | tf_op jit(solution)/shard_map/psum | solution.py:42
  197.1 406.4 %all-reduce.22.cloned.1.call-start = ((), (), s32[]{:S(2)}) async-start(), calls=%async_computation.4 | async-start | bytes 1048576 | tf_op jit(solution)/shard_map/psum | solution.py:42
  456.0 304.9 %all-reduce.20.cloned.1.call-start = ((), (), s32[]{:S(2)}) async-start(), calls=%async_computation.3 | async-start | bytes 1048576 | tf_op jit(solution)/shard_map/psum | solution.py:42
  608.3 406.4 %all-reduce.18.cloned.1.call-start = ((), (), s32[]{:S(2)}) async-start(), calls=%async_computation.2 | async-start | bytes 1048576 | tf_op jit(solution)/shard_map/psum | solution.py:42
  867.2 304.9 %all-reduce.16.cloned.1.call-start = ((), (), s32[]{:S(2)}) async-start(), calls=%async_computation.1 | async-start | bytes 1048576 | tf_op jit(solution)/shard_map/psum | solution.py:42
Sparse Core Ops, SparseCore 0:
  45.5 146.6 all-reduce.25
  197.2 152.5 all-reduce.23
  456.1 147.2 all-reduce.21
  608.4 152.4 all-reduce.19
  867.3 147.3 all-reduce.17
  1019.6 152.4 all-reduce.15
